TPU v7x, 128 devices: a whole 4x4x4 slice. The times are simulated.
128 devices in a mesh: seq: 16 (over x, y), exp: 8 (over z, core).
Axes of the slice: x: 4, y: 4, z: 4, core: 2. Of those that a mesh axis runs over, the one named last changes fastest.
Arguments:
- hidden: bfloat16 [2048, 4096], P('seq', 'exp'), may hold values from -6 to 6
- queries: bfloat16 [2048, 4096], P('seq', 'exp'), may hold values from -40 to 40
- keys: bfloat16 [2048, 1024], P('seq', 'exp'), may hold values from -6 to 6
- values: bfloat16 [2048, 1024], P('seq', 'exp'), may hold values from -6 to 6
- block_place: int32 [32], replicated, may hold values from 0 to 31, as said below
- page_table: int32 [128], replicated, may hold values from 0 to 127, each once
- out_weight: bfloat16 [4096, 4096], P('exp'), may hold values from -0.09375 to 0.09375
- norm_gain: float32 [4096], replicated, may hold values from 0.5 to 2
- gate_probs: float32 [2048, 2], P('seq'), may hold values from 0.1 to 1
- routes: int32 [2048, 2], P('seq'), may hold values from 0 to 7, all different within a row; in each aligned block of 128 rows (0 to 127, 128 to 255, ...) at most 64 rows name the same one
- w_gate: bfloat16 [8, 4096, 14336], P('exp', None, 'seq'), may hold values from -0.09375 to 0.09375
- w_up: bfloat16 [8, 4096, 14336], P('exp', None, 'seq'), may hold values from -0.09375 to 0.09375
- w_down: bfloat16 [8, 14336, 4096], P('exp', 'seq'), may hold values from -0.046875 to 0.046875
Outputs:
- layer_out: bfloat16 [2048, 4096], P('seq', 'exp')
- key_value_pages: bfloat16 [128, 16, 2, 1024], P('seq', None, None, 'exp')
Inputs may be any that keep to these rules, and one draw needn't show every extreme that they name: `block_place`: the first 24 entries are a permutation of 0 to 23, the others a permutation of 24 to 31. `page_table`: A permutation of the pages. `routes`: in the rows of one index of seq (128 rows) no expert is named more than 64 times, a bound that some block reaches; a row names two different experts.
All inputs are finite; a program needn't handle non-finite values.
Results may differ from a plain program's by a relative error of at most 0.02.
Values may be sent and summed in bfloat16 or wider, within the bound.
No kernel may reach another device: no remote copies, remote signals or barrier semaphores. Data moves between devices by JAX's collectives and lax.ppermute only.
A program may use at most 128 MiB of HBM per device.

v0:
```python
import math
import jax
import jax.numpy as jnp
from jax import lax
from jax.sharding import PartitionSpec as P

HEAD_SIZE = 128
NEXP = 8
PAGE_TOKENS = 16
THETA = 1000000.0
EPS = 1e-05


def apply_rotary(values_in, positions, head_count):
    row_count = values_in.shape[0]
    split_view = values_in.astype(jnp.float32).reshape(row_count, head_count, HEAD_SIZE)
    steps_half = jnp.arange(HEAD_SIZE // 2, dtype=jnp.float32)
    frequency = THETA ** (-(2.0 * steps_half) / HEAD_SIZE)
    angles = positions.astype(jnp.float32)[:, None] * frequency[None, :]
    cosine = jnp.cos(angles)[:, None, :]
    sine_part = jnp.sin(angles)[:, None, :]
    front_half = split_view[..., : HEAD_SIZE // 2]
    back_half = split_view[..., HEAD_SIZE // 2 :]
    turned = jnp.concatenate(
        [front_half * cosine - back_half * sine_part, back_half * cosine + front_half * sine_part],
        axis=-1,
    )
    return turned.reshape(row_count, head_count * HEAD_SIZE).astype(jnp.bfloat16)


def per_device(
    hidden,
    queries,
    keys,
    values,
    block_place,
    page_table,
    out_weight,
    norm_gain,
    gate_probs,
    routes,
    w_gate,
    w_up,
    w_down,
):
    seq_count = lax.axis_size("seq")
    exp_count = lax.axis_size("exp")
    seq_index = lax.axis_index("seq")
    tok_rows = queries.shape[0]
    half_rows = tok_rows // 2
    all_rows = tok_rows * seq_count
    long_len = 3 * all_rows // 4
    every_row = jnp.arange(all_rows, dtype=jnp.int32)
    all_pos = block_place[every_row // half_rows] * half_rows + every_row % half_rows
    my_pos = lax.dynamic_slice_in_dim(all_pos, seq_index * tok_rows, tok_rows)
    my_long = my_pos >= long_len
    my_rope = my_pos - long_len * my_long.astype(jnp.int32)
    q_heads = queries.shape[1] // HEAD_SIZE
    kv_heads = keys.shape[1] // HEAD_SIZE
    query_head_group = q_heads // kv_heads
    query_rotated = apply_rotary(queries, my_rope, q_heads)
    key_rotated = apply_rotary(keys, my_rope, kv_heads)
    q_grid = query_rotated.reshape(tok_rows, kv_heads, query_head_group, HEAD_SIZE)
    score_scale = 1.0 / math.sqrt(HEAD_SIZE)
    page_count = tok_rows // PAGE_TOKENS
    inverse_table = jnp.argsort(page_table)
    my_logical = lax.dynamic_slice_in_dim(inverse_table, seq_index * page_count, page_count)
    row_at = jnp.argsort(all_pos)
    taken = row_at[
        (
            my_logical[:, None] * PAGE_TOKENS + jnp.arange(PAGE_TOKENS, dtype=jnp.int32)[None, :]
        ).reshape(page_count * PAGE_TOKENS)
    ]
    key_all, value_all = (
        lax.all_gather(key_rotated, "seq", axis=0, tiled=True),
        lax.all_gather(values, "seq", axis=0, tiled=True),
    )
    peak_old = jnp.full((kv_heads, query_head_group, tok_rows), -1e30, jnp.float32)
    row_count = key_all.shape[0]
    scores = (
        jnp.einsum(
            "tkgd,nkd->kgtn",
            q_grid,
            key_all.reshape(row_count, kv_heads, HEAD_SIZE),
            preferred_element_type=jnp.float32,
        )
        * score_scale
    )
    allowed = ((all_pos >= long_len)[None, :] == my_long[:, None]) & (
        all_pos[None, :] <= my_pos[:, None]
    )
    scores = jnp.where(allowed, scores, -1e30)
    peak_new = jnp.maximum(peak_old, jnp.max(scores, axis=-1))
    weights = jnp.where(allowed, jnp.exp(scores - peak_new[..., None]), 0.0)
    total_new = jnp.sum(weights, axis=-1)
    summed = jnp.einsum(
        "kgtn,nkd->kgtd",
        weights.astype(jnp.bfloat16),
        value_all.reshape(row_count, kv_heads, HEAD_SIZE),
        preferred_element_type=jnp.float32,
    )
    peak_final, total_final, summed = (peak_new, total_new, summed)
    cache_pages = jnp.stack([key_all[taken], value_all[taken]], axis=1).reshape(
        page_count, PAGE_TOKENS, 2, kv_heads * HEAD_SIZE
    )
    attended = (
        (summed / total_final[..., None])
        .transpose(2, 0, 1, 3)
        .reshape(tok_rows, q_heads * HEAD_SIZE)
        .astype(jnp.bfloat16)
    )
    partial_proj = jnp.dot(attended, out_weight, preferred_element_type=jnp.float32)
    projected = lax.psum_scatter(
        partial_proj.astype(jnp.bfloat16), "exp", scatter_dimension=1, tiled=True
    ).astype(jnp.float32)
    residual = (hidden.astype(jnp.float32) + projected).astype(jnp.bfloat16)
    top_count = routes.shape[1]
    capacity = tok_rows // 2
    assign_count = tok_rows * top_count
    flat_routes = routes.reshape(assign_count)
    expert_hot = (flat_routes[:, None] == jnp.arange(NEXP, dtype=jnp.int32)[None, :]).astype(
        jnp.float32
    )
    earlier = (jnp.arange(assign_count)[:, None] > jnp.arange(assign_count)[None, :]).astype(
        jnp.float32
    )
    before = jnp.dot(earlier, expert_hot, preferred_element_type=jnp.float32)
    slot_rank = jnp.sum(before * expert_hot, axis=1).astype(jnp.int32).reshape(tok_rows, top_count)
    slot_grid = routes * capacity + slot_rank
    chooser = jnp.any(
        slot_grid[None, :, :] == jnp.arange(NEXP * capacity, dtype=jnp.int32)[:, None, None],
        axis=-1,
    ).astype(jnp.bfloat16)
    outgoing_rows = jnp.dot(chooser, residual, preferred_element_type=jnp.float32).astype(
        jnp.bfloat16
    )
    expert_local = NEXP // exp_count
    arrived_rows = lax.all_to_all(
        outgoing_rows.reshape(exp_count, expert_local * capacity, -1),
        "exp",
        split_axis=0,
        concat_axis=2,
        tiled=True,
    )
    gathered_in = arrived_rows.astype(jnp.float32)
    mean_square = jnp.mean(gathered_in * gathered_in, axis=-1, keepdims=True)
    normed = (gathered_in * lax.rsqrt(mean_square + EPS) * norm_gain).astype(jnp.bfloat16)
    token_rows = lax.all_gather(normed, "seq", axis=1, tiled=True)
    gate_part = jnp.einsum("end,edf->enf", token_rows, w_gate, preferred_element_type=jnp.float32)
    up_part = jnp.einsum("end,edf->enf", token_rows, w_up, preferred_element_type=jnp.float32)
    hidden_units = (jax.nn.silu(gate_part) * up_part).astype(jnp.bfloat16)
    returned = lax.psum_scatter(
        jnp.einsum("enf,efd->ned", hidden_units, w_down, preferred_element_type=jnp.float32).astype(
            jnp.bfloat16
        ),
        "seq",
        scatter_dimension=0,
        tiled=True,
    )
    homed = lax.all_to_all(returned, "exp", split_axis=2, concat_axis=1, tiled=True)
    lookup = homed.reshape(capacity * NEXP, -1)
    chosen = (
        lookup[(slot_rank * NEXP + routes).reshape(assign_count)]
        .astype(jnp.float32)
        .reshape(tok_rows, top_count, -1)
    )
    gate_share = gate_probs / jnp.sum(gate_probs, axis=1, keepdims=True)
    layer_out = (
        residual.astype(jnp.float32) + jnp.sum(gate_share[:, :, None] * chosen, axis=1)
    ).astype(jnp.bfloat16)
    return (layer_out, cache_pages)


def solution(mesh):
    return jax.shard_map(
        per_device,
        mesh=mesh,
        in_specs=(
            P("seq", "exp"),
            P("seq", "exp"),
            P("seq", "exp"),
            P("seq", "exp"),
            P(),
            P(),
            P("exp", None),
            P(),
            P("seq", None),
            P("seq", None),
            P("exp", None, "seq"),
            P("exp", None, "seq"),
            P("exp", "seq", None),
        ),
        out_specs=(P("seq", "exp"), P("seq", None, None, "exp")),
        check_vma=False,
    )
```

profile of v0, /device:TPU:1, one launch (start us, length us, event | category | flops | bytes accessed | tf_op | source)
XLA Modules:
  0.0 390.9 jit_solution(8095771630104824144)
XLA Ops:
  8.4 1.8 fusion.55
  10.2 2.1 fusion.54
  12.3 4.3 %compare_select_fusion.1 = s32[2048,1]{0,1:T(1,128)S(1)} fusion(s32[]{:T(128)} %bitcast.25, s32[]{:T(128)} %bitcast.26, s32[]{:T(128)} %bitcast.27, s32[]{:T(128)} %bitcast.28, s32[]{:T(128)} %bitcast.29, s32[]{:T(128)} %bitcast.31, s32[]{:T(128)} %bitcast.30), kind=kLoop, calls=%fused_computation.88 | loop fusion | flops 47104 | bytes 8220 | tf_op jit(solution)/shard_map/gather | solution.py:54
  16.7 15.8 %broadcast_compare_fusion = (pred[2048]{0:T(1024)(128)(4,1)S(1)}, s32[2048]{0:T(1024)S(1)}) fusion(pred[2048]{0:T(1024)(128)(4,1)S(1)} %compare_reduce_fusion, pred[2048]{0:T(1024)(128)(4,1)S(1)} %compare_reduce_fusion.1, pred[2048]{0:T(1024)(128)(4,1)S(1)} %compare_reduce_fusion.2, pred[2048]{0:T(1024)(128)(4,1)S(1)} %compare_reduce_fusion.3, ...), kind=kLoop, calls=%fused_computation.112 | loop fusion | flops 69632 | bytes 69732 | tf_op jit(solution)/shard_map/ge | solution.py:89
  32.4 0.1 broadcast_compare_fusion.1
  32.5 0.9 copy.61
  33.4 0.3 multiply_cosine_fusion
  33.7 0.2 fusion.38
  33.9 1.0 copy.62
  35.0 0.1 copy.78
  35.1 0.1 copy.77
  35.3 20.5 %all-gather = bf16[2048,1,128]{0,2,1:T(8,128)(2,1)S(1)} all-gather(bf16[128,1,128]{0,2,1:T(8,128)(2,1)S(1)} %pad_maximum_fusion.1), channel_id=2, replica_groups=mesh['seq'=16,'exp'=8] {'seq'}, dimensions={0}, use_global_device_ids=true | all-gather | bytes 557056 | tf_op jit(solution)/shard_map/all_gather | solution.py:75
  55.8 18.2 %all_gather.10 = bf16[2048,128]{1,0:T(8,128)(2,1)S(1)} all-gather(bf16[128,128]{1,0:T(8,128)(2,1)} %param.16), channel_id=1, replica_groups=mesh['seq'=16,'exp'=8] {'seq'}, dimensions={0}, use_global_device_ids=true | all-gather | bytes 557056 | tf_op jit(solution)/shard_map/all_gather | solution.py:76
  74.0 1.5 compare_and_fusion
  75.5 0.1 subtract_convert_fusion
  75.6 0.8 fusion.7
  76.5 1.0 fusion.8
  77.5 1.1 fusion.22
  78.6 1.1 copy-done
  79.7 1.7 convolution_convert_fusion
  81.5 0.1 copy.67
  81.6 0.1 eq.46
  81.8 0.2 fusion.18
  82.0 0.1 convert_element_type.133
  82.2 0.1 fusion.29
  82.3 39.0 %reduce-scatter.3.cloned.1.call-done = bf16[128,512]{1,0:T(8,128)(2,1)} async-done(((bf16[128,4096]{1,0:T(8,128)(2,1)}), bf16[128,512]{1,0:T(8,128)(2,1)}) %reduce-scatter.3.cloned.1.call-update) | async-done | bytes 131088 | tf_op jit(solution)/shard_map/reduce_scatter | solution.py:113
  121.3 1.2 convolution_convert_fusion.1
  122.5 15.3 %all_to_all.8 = bf16[8,64,512]{2,1,0:T(8,128)(2,1)S(1)} all-to-all(bf16[8,64,512]{2,1,0:T(8,128)(2,1)S(1)} %bitcast.130), channel_id=1, replica_groups=mesh['seq'=16,'exp'=8] {'exp'}, dimensions={0} | all-to-all | bytes 1048576 | tf_op jit(solution)/shard_map/all_to_all | solution.py:138
  137.8 0.2 fusion.25
  138.0 0.1 convert_bitcast_fusion.1
  138.1 0.1 copy.79
  138.3 1.0 multiply_convert_fusion.1
  139.3 0.2 reduce-scatter.5.cloned.1.call-start
  139.5 70.0 %all-gather.3.cloned.1.call-done = bf16[1,1024,4096]{2,1,0:T(8,128)(2,1)} async-done(((bf16[1,64,4096]{2,1,0:T(8,128)(2,1)}), bf16[1,1024,4096]{2,1,0:T(8,128)(2,1)}) %all-gather.3.cloned.1.call-update) | async-done | bytes 8388624 | tf_op jit(solution)/shard_map/all_gather | solution.py:148
  209.5 12.5 %fusion = f32[1024,896]{1,0:T(8,128)S(1)} fusion(bf16[1,1024,4096]{2,1,0:T(8,128)(2,1)} %all-gather.3.cloned.1.call-done, bf16[1,4096,896]{2,1,0:T(8,128)(2,1)} %param.24), kind=kOutput, calls=%fused_computation.4 | convolution fusion | flops 7516192768 | bytes 19398656 | tf_op jit(solution)/shard_map/end,edf->enf/dot_general | solution.py:150
  222.0 12.1 %multiply_convert_fusion = bf16[1024,896]{1,0:T(8,128)(2,1)S(1)} fusion(f32[1024,896]{1,0:T(8,128)S(1)} %fusion, bf16[1,4096,896]{2,1,0:T(8,128)(2,1)} %param.23, bf16[1,1024,4096]{2,1,0:T(8,128)(2,1)S(1)} %copy-done.6), kind=kOutput, calls=%fused_computation.16 | convolution fusion | flops 7521697792 | bytes 21233664 | tf_op jit(solution)/shard_map/end,edf->enf/dot_general | solution.py:149
  234.1 11.1 %convert_bitcast_fusion = bf16[1024,1,4096]{2,0,1:T(8,128)(2,1)} fusion(bf16[1024,896]{1,0:T(8,128)(2,1)S(1)} %multiply_convert_fusion, bf16[1,896,4096]{2,1,0:T(8,128)(2,1)S(1)} %bitcast.138), kind=kOutput, calls=%fused_computation.8 | convolution fusion | flops 7520387072 | bytes 17563648 | tf_op jit(solution)/shard_map/enf,efd->ned/dot_general | solution.py:153
  245.2 0.6 copy-done.7
  245.9 2.5 sort.35
  248.4 0.1 dynamic-slice_multiply_fusion
  248.5 0.1 iota_add_fusion
  248.5 0.1 add.166
  248.6 5.0 %sort.34 = (s32[2048]{0:T(1024)}, s32[2048]{0:T(1024)S(1)}) sort(s32[2048]{0:T(1024)S(1)} %get-tuple-element.7, s32[2048]{0:T(1024)S(1)} %iota.49), dimensions={0}, to_apply=%region_9.10 | sort | flops 22528 | bytes 32768 | tf_op jit(solution)/shard_map/jit(argsort)/sort | solution.py:68
  253.7 1.1 gather_fusion.1
  254.9 74.9 %reduce-scatter.5.cloned.1.call-done = bf16[64,1,4096]{2,0,1:T(8,128)(2,1)} async-done(((bf16[1024,1,4096]{2,0,1:T(8,128)(2,1)}), bf16[64,1,4096]{2,0,1:T(8,128)(2,1)}) %reduce-scatter.5.cloned.1.call-update) | async-done | bytes 524304 | tf_op jit(solution)/shard_map/reduce_scatter | solution.py:152
  329.8 4.9 %copy.70 = bf16[64,1,4096]{0,1,2:T(2,128)(2,1)S(1)} copy(bf16[64,1,4096]{2,0,1:T(8,128)(2,1)} %reduce-scatter.5.cloned.1.call-done) | data formatting | bytes 1048576 | tf_op jit(solution)/shard_map/reduce_scatter | solution.py:152
  334.7 0.5 broadcast.624
  335.2 23.6 %reduce.56 = bf16[4096,64]{1,0:T(8,128)(2,1)} reduce(bf16[4096,1,64]{2,1,0:T(2,128)(2,1)S(1)} %bitcast.127, bf16[]{:T(256)} %broadcast.624), dimensions={1}, to_apply=%bitcast.118.reduce_sub_computation | reduce | bytes 1048578
  358.8 3.0 reshape.625
  361.8 6.6 %all-to-all-start.1 = ((bf16[8,2,16384]{2,1,0:T(2,128)(2,1)}), bf16[8,2,16384]{2,1,0:T(2,128)(2,1)S(1)}, u32[]{:S(2)}, u32[]{:S(2)}) async-start(bf16[8,2,16384]{2,1,0:T(2,128)(2,1)} %reshape.625), calls=%async_computation.3 | async-start | bytes 1048576 | tf_op jit(solution)/shard_map/all_to_all | solution.py:160
  368.4 0.1 copy.66
  368.5 0.1 reshape.441
  368.6 0.7 gather_fusion.3
  369.4 0.3 copy.73
  369.7 0.7 gather_fusion.2
  370.5 0.8 pad_maximum_fusion
  371.3 6.5 %all-to-all-done.1 = bf16[8,2,16384]{2,1,0:T(2,128)(2,1)S(1)} async-done(((bf16[8,2,16384]{2,1,0:T(2,128)(2,1)}), bf16[8,2,16384]{2,1,0:T(2,128)(2,1)S(1)}, u32[]{:S(2)}, u32[]{:S(2)}) %all-to-all-start.1) | async-done | bytes 524320 | tf_op jit(solution)/shard_map/all_to_all | solution.py:160
  377.7 1.2 reshape.626
  379.0 2.3 copy.71
  381.2 0.2 reshape.440
  381.5 1.2 gather_fusion
  382.6 0.3 reshape.447
  383.0 0.7 multiply_reduce_fusion
  383.7 0.7 add_convert_fusion
  (72 shorter events, 1.6 us)
Async XLA Ops:
  7.2 114.1 %reduce-scatter.3.cloned.1.call-start = ((), (), s32[]{:S(2)}) async-start(), calls=%async_computation.4 | async-start | bytes 1179648 | tf_op jit(solution)/shard_map/reduce_scatter | solution.py:113
  77.5 2.2 copy-start
  78.6 2.9 copy-start.4
  78.6 42.7 %copy-start.1 = (bf16[128,512]{1,0:T(8,128)(2,1)S(1)}, bf16[128,512]{1,0:T(8,128)(2,1)}, u32[]{:S(2)}) copy-start(bf16[128,512]{1,0:T(8,128)(2,1)} %param.13) | copy-start | bytes 393220
  81.4 56.8 %copy-start.3 = (f32[4096]{0:T(1024)S(1)}, f32[4096]{0:T(1024)}, u32[]{:S(2)}) copy-start(f32[4096]{0:T(1024)} %param.20) | copy-start | bytes 49156
  81.4 128.1 %all-gather.3.cloned.1.call-start = ((), (), s32[]{:S(2)}) async-start(), calls=%async_computation.5 | async-start | bytes 8912896 | tf_op jit(solution)/shard_map/all_gather | solution.py:148
  139.3 190.5 %reduce-scatter.5.cloned.1.call-start = ((), (), s32[]{:S(2)}) async-start(), calls=%async_computation.6 | async-start | bytes 8912896 | tf_op jit(solution)/shard_map/reduce_scatter | solution.py:152
  209.5 12.5 %copy-start.6 = (bf16[1,1024,4096]{2,1,0:T(8,128)(2,1)S(1)}, bf16[1,1024,4096]{2,1,0:T(8,128)(2,1)}, u32[]{:S(2)}) copy-start(bf16[1,1024,4096]{2,1,0:T(8,128)(2,1)} %all-gather.3.cloned.1.call-done) | copy-start | bytes 25165828
  209.5 24.6 %slice-start = ((s8[7340032]{0:T(1024)(128)(4,1)}), s8[4194304]{0:T(1024)(128)(4,1)S(1)}, s32[]{:S(2)}) async-start(s8[7340032]{0:T(1024)(128)(4,1)} %bitcast.137), calls=%async_computation.7 | async-start | bytes 8388608
  222.0 12.1 %slice-start.1 = ((s8[7340032]{0:T(1024)(128)(4,1)}), s8[3145728]{0:T(1024)(128)(4,1)S(1)}, s32[]{:S(2)}) async-start(s8[7340032]{0:T(1024)(128)(4,1)} %bitcast.137), calls=%async_computation.8 | async-start | bytes 6291456
  245.2 0.7 copy-start.7
  245.2 8.5 %copy-start.5 = (f32[128,2]{0,1:T(2,128)S(1)}, f32[128,2]{0,1:T(2,128)}, u32[]{:S(2)}) copy-start(f32[128,2]{0,1:T(2,128)} %param.21) | copy-start | bytes 3076
  361.8 15.9 %all-to-all-start.1 = ((bf16[8,2,16384]{2,1,0:T(2,128)(2,1)}), bf16[8,2,16384]{2,1,0:T(2,128)(2,1)S(1)}, u32[]{:S(2)}, u32[]{:S(2)}) async-start(bf16[8,2,16384]{2,1,0:T(2,128)(2,1)} %reshape.625), calls=%async_computation.3 | async-start | bytes 1048576 | tf_op jit(solution)/shard_map/all_to_all | solution.py:160
  379.0 4.7 %copy-start.2 = (bf16[128,512]{1,0:T(8,128)(2,1)S(1)}, bf16[128,512]{1,0:T(8,128)(2,1)}, u32[]{:S(2)}) copy-start(bf16[128,512]{1,0:T(8,128)(2,1)} %reduce-scatter.3.cloned.1.call-done) | copy-start | bytes 393220
Sparse Core Ops, SparseCore 0:
  81.6 39.6 reduce-scatter.2
  139.4 70.0 all-gather.2
  245.4 84.3 reduce-scatter.4
where the time goes:
time: 392 us; the launch traced here: 391 us
  waiting for transfers between devices  190 us (48%)
  other arithmetic  59.5 us (15%)
  blocking collectives  54.1 us (14%)
  matrix products  40.6 us (10%)
  local copies, waits for them, and re-layouts  25.3 us (6%)
  between operations  14.2 us (4%)
  starting transfers between devices  6.86 us (2%)
    reduce_scatter x1, waiting for transfers between devices, per_device(): lax.psum_scatter(jnp.einsum('enf,efd->ned', hidden_units, w_down, preferr...  74.9 us
    all_gather x1, waiting for transfers between devices, per_device(): token_rows = lax.all_gather(normed, 'seq', axis=1, tiled=True)  70 us
    reduce_scatter x1, waiting for transfers between devices, per_device(): lax.psum_scatter(partial_proj.astype(jnp.bfloat16), 'exp', scatter_dimens...  39 us
    unnamed x3, other arithmetic  23.7 us
    all_gather x1, blocking collectives, per_device(): lax.all_gather(key_rotated, 'seq', axis=0, tiled=True)  20.5 us
    all_gather x1, blocking collectives, per_device(): lax.all_gather(values, 'seq', axis=0, tiled=True)  18.2 us
    ge x1, other arithmetic, per_device(): all_pos >= long_len  15.8 us
    all_to_all x1, blocking collectives, per_device(): lax.all_to_all(outgoing_rows.reshape(exp_count, expert_local * capacity,...  15.3 us
  transfers between devices with their start and end apart: 4, of which 4 were waited for; matrix products, arithmetic and copies ran while one was open for 3% of the time, Pallas kernels for 0%

commit v1 on v0

--- a/solution.py
+++ b/solution.py
@@ -9,6 +9,22 @@
 PAGE_TOKENS = 16
 THETA = 1000000.0
 EPS = 1e-05
+
+
+def exchange_in_pairs(x, axis, split, join):
+    ways, here = (lax.axis_size(axis), lax.axis_index(axis))
+    width = x.shape[split] // ways
+    shape = list(x.shape)
+    shape[split] = width
+    height = shape[join]
+    shape[join] = height * ways
+    full = jnp.zeros(shape, x.dtype)
+    for mask in range(ways):
+        part = lax.dynamic_slice_in_dim(x, (here ^ mask) * width, width, axis=split)
+        if mask:
+            part = lax.ppermute(part, axis, [(d, d ^ mask) for d in range(ways)])
+        full = lax.dynamic_update_slice_in_dim(full, part, (here ^ mask) * height, axis=join)
+    return full
 
 
 def apply_rotary(values_in, positions, head_count):
@@ -157,7 +173,7 @@
         scatter_dimension=0,
         tiled=True,
     )
-    homed = lax.all_to_all(returned, "exp", split_axis=2, concat_axis=1, tiled=True)
+    homed = exchange_in_pairs(returned, "exp", 2, 1)
     lookup = homed.reshape(capacity * NEXP, -1)
     chosen = (
         lookup[(slot_rank * NEXP + routes).reshape(assign_count)]

time: 392 us -> 361 us (0.921)
  other arithmetic: 59.5 us -> 35.9 us
  local copies, waits for them, and re-layouts: 25.3 us -> 15.8 us
    unnamed x3 -> x2, other arithmetic: 23.7 us -> 0.13 us
    ppermute x0 -> x7, waiting for transfers between devices: none -> 9.4 us  [exchange_in_pairs(): part = lax.ppermute(part, axis, [(d, d ^ mask) for d in range(ways)])]
    ppermute x0 -> x7, starting transfers between devices: none -> 8.9 us  [exchange_in_pairs(): part = lax.ppermute(part, axis, [(d, d ^ mask) for d in range(ways)])]
    all_to_all x1 -> x0, starting transfers between devices: 6.55 us -> none  [per_device(): lax.all_to_all(returned, 'exp', split_axis=2, concat_axis=1, tiled=True)]
    all_to_all x1 -> x0, waiting for transfers between devices: 6.46 us -> none  [per_device(): lax.all_to_all(returned, 'exp', split_axis=2, concat_axis=1, tiled=True)]
    reduce_scatter x1 -> x0, local copies, waits for them, and re-layouts: 4.86 us -> none  [per_device(): lax.psum_scatter(jnp.einsum('enf,efd->ned', hidden_units, w_down, preferr...]
    unnamed x28 -> x25, local copies, waits for them, and re-layouts: 8.75 us -> 3.91 us
  transfers between devices with their start and end apart: 4 -> 10, of which waited for: 4 -> 5; matrix products, arithmetic and copies ran while one was open for 3% -> 4% of each run, Pallas kernels for 0% -> 0%
where the time goes in v1:
time: 361 us; the launch traced here: 360 us
  waiting for transfers between devices  190 us (53%)
  blocking collectives  54.1 us (15%)
  matrix products  40.7 us (11%)
  other arithmetic  35.9 us (10%)
  local copies, waits for them, and re-layouts  15.8 us (4%)
  between operations  14.4 us (4%)
  starting transfers between devices  9.2 us (3%)
    reduce_scatter x1, waiting for transfers between devices, per_device(): lax.psum_scatter(jnp.einsum('enf,efd->ned', hidden_units, w_down, preferr...  71.8 us
    all_gather x1, waiting for transfers between devices, per_device(): token_rows = lax.all_gather(normed, 'seq', axis=1, tiled=True)  70 us
    reduce_scatter x1, waiting for transfers between devices, per_device(): lax.psum_scatter(partial_proj.astype(jnp.bfloat16), 'exp', scatter_dimens...  39 us
    all_gather x1, blocking collectives, per_device(): lax.all_gather(key_rotated, 'seq', axis=0, tiled=True)  20.5 us
    all_gather x1, blocking collectives, per_device(): lax.all_gather(values, 'seq', axis=0, tiled=True)  18.2 us
    ge x1, other arithmetic, per_device(): all_pos >= long_len  15.8 us
    all_to_all x1, blocking collectives, per_device(): lax.all_to_all(outgoing_rows.reshape(exp_count, expert_local * capacity,...  15.3 us
    dot_general x1, matrix products, per_device(): jnp.einsum('end,edf->enf', token_rows, w_up, preferred_element_type=jnp.f...  12.5 us
  transfers between devices with their start and end apart: 10, of which 5 were waited for; matrix products, arithmetic and copies ran while one was open for 4% of the time, Pallas kernels for 0%

profile of v1, /device:TPU:1, one launch (start us, length us, event | category | flops | bytes accessed | tf_op | source)
XLA Modules:
  0.0 360.3 jit_solution(15924470454836005255)
XLA Ops:
  8.4 1.8 fusion.55
  10.2 2.1 fusion.54
  12.3 4.3 %compare_select_fusion.1 = s32[2048,1]{0,1:T(1,128)S(1)} fusion(s32[]{:T(128)} %bitcast.25, s32[]{:T(128)} %bitcast.26, s32[]{:T(128)} %bitcast.27, s32[]{:T(128)} %bitcast.28, s32[]{:T(128)} %bitcast.29, s32[]{:T(128)} %bitcast.31, s32[]{:T(128)} %bitcast.30), kind=kLoop, calls=%fused_computation.89 | loop fusion | flops 47104 | bytes 8220 | tf_op jit(solution)/shard_map/gather | solution.py:70
  16.7 15.8 %broadcast_compare_fusion = (pred[2048]{0:T(1024)(128)(4,1)S(1)}, s32[2048]{0:T(1024)S(1)}) fusion(pred[2048]{0:T(1024)(128)(4,1)S(1)} %compare_reduce_fusion, pred[2048]{0:T(1024)(128)(4,1)S(1)} %compare_reduce_fusion.1, pred[2048]{0:T(1024)(128)(4,1)S(1)} %compare_reduce_fusion.2, pred[2048]{0:T(1024)(128)(4,1)S(1)} %compare_reduce_fusion.3, ...), kind=kLoop, calls=%fused_computation.113 | loop fusion | flops 69632 | bytes 69732 | tf_op jit(solution)/shard_map/ge | solution.py:105
  32.4 0.1 broadcast_compare_fusion.1
  32.5 0.9 copy.65
  33.4 0.3 multiply_cosine_fusion
  33.7 0.2 fusion.38
  33.9 1.0 copy.66
  35.0 0.1 copy.82
  35.1 0.1 copy.81
  35.3 20.5 %all-gather = bf16[2048,1,128]{0,2,1:T(8,128)(2,1)S(1)} all-gather(bf16[128,1,128]{0,2,1:T(8,128)(2,1)S(1)} %pad_maximum_fusion.1), channel_id=2, replica_groups=mesh['seq'=16,'exp'=8] {'seq'}, dimensions={0}, use_global_device_ids=true | all-gather | bytes 557056 | tf_op jit(solution)/shard_map/all_gather | solution.py:91
  55.8 18.2 %all_gather.10 = bf16[2048,128]{1,0:T(8,128)(2,1)S(1)} all-gather(bf16[128,128]{1,0:T(8,128)(2,1)} %param.16), channel_id=1, replica_groups=mesh['seq'=16,'exp'=8] {'seq'}, dimensions={0}, use_global_device_ids=true | all-gather | bytes 557056 | tf_op jit(solution)/shard_map/all_gather | solution.py:92
  74.1 1.5 compare_and_fusion
  75.5 0.1 subtract_convert_fusion
  75.6 0.8 fusion.7
  76.5 1.0 fusion.8
  77.5 1.1 fusion.22
  78.6 1.1 copy-done
  79.7 1.7 convolution_convert_fusion
  81.5 0.1 copy.71
  81.6 0.1 eq.46
  81.8 0.2 fusion.18
  82.0 0.1 convert_element_type.133
  82.3 39.0 %reduce-scatter.3.cloned.1.call-done = bf16[128,512]{1,0:T(8,128)(2,1)} async-done(((bf16[128,4096]{1,0:T(8,128)(2,1)}), bf16[128,512]{1,0:T(8,128)(2,1)}) %reduce-scatter.3.cloned.1.call-update) | async-done | bytes 131088 | tf_op jit(solution)/shard_map/reduce_scatter | solution.py:129
  121.3 1.2 convolution_convert_fusion.1
  122.5 15.3 %all_to_all.4 = bf16[8,64,512]{2,1,0:T(8,128)(2,1)S(1)} all-to-all(bf16[8,64,512]{2,1,0:T(8,128)(2,1)S(1)} %bitcast.126), channel_id=1, replica_groups=mesh['seq'=16,'exp'=8] {'exp'}, dimensions={0} | all-to-all | bytes 1048576 | tf_op jit(solution)/shard_map/all_to_all | solution.py:154
  137.8 0.2 fusion.25
  138.0 0.1 convert_bitcast_fusion.1
  138.2 0.1 copy.83
  138.3 1.0 multiply_convert_fusion.1
  139.3 0.2 reduce-scatter.5.cloned.1.call-start
  139.5 70.0 %all-gather.3.cloned.1.call-done = bf16[1,1024,4096]{2,1,0:T(8,128)(2,1)} async-done(((bf16[1,64,4096]{2,1,0:T(8,128)(2,1)}), bf16[1,1024,4096]{2,1,0:T(8,128)(2,1)}) %all-gather.3.cloned.1.call-update) | async-done | bytes 8388624 | tf_op jit(solution)/shard_map/all_gather | solution.py:164
  209.5 12.5 %fusion = f32[1024,896]{1,0:T(8,128)S(1)} fusion(bf16[1,1024,4096]{2,1,0:T(8,128)(2,1)} %all-gather.3.cloned.1.call-done, bf16[1,4096,896]{2,1,0:T(8,128)(2,1)} %param.24), kind=kOutput, calls=%fused_computation.4 | convolution fusion | flops 7516192768 | bytes 19398656 | tf_op jit(solution)/shard_map/end,edf->enf/dot_general | solution.py:166
  222.0 12.1 %multiply_convert_fusion = bf16[1024,896]{1,0:T(8,128)(2,1)S(1)} fusion(f32[1024,896]{1,0:T(8,128)S(1)} %fusion, bf16[1,4096,896]{2,1,0:T(8,128)(2,1)} %param.23, bf16[1,1024,4096]{2,1,0:T(8,128)(2,1)S(1)} %copy-done.6), kind=kOutput, calls=%fused_computation.16 | convolution fusion | flops 7521697792 | bytes 21233664 | tf_op jit(solution)/shard_map/end,edf->enf/dot_general | solution.py:165
  234.1 11.1 %convert_bitcast_fusion = bf16[1024,1,4096]{2,0,1:T(8,128)(2,1)} fusion(bf16[1024,896]{1,0:T(8,128)(2,1)S(1)} %multiply_convert_fusion, bf16[1,896,4096]{2,1,0:T(8,128)(2,1)S(1)} %bitcast.134), kind=kOutput, calls=%fused_computation.8 | convolution fusion | flops 7520387072 | bytes 17563648 | tf_op jit(solution)/shard_map/enf,efd->ned/dot_general | solution.py:169
  245.3 0.5 copy-done.7
  245.9 2.5 sort.35
  248.6 5.0 %sort.34 = (s32[2048]{0:T(1024)}, s32[2048]{0:T(1024)S(1)}) sort(s32[2048]{0:T(1024)S(1)} %get-tuple-element.7, s32[2048]{0:T(1024)S(1)} %iota.49), dimensions={0}, to_apply=%region_9.10 | sort | flops 22528 | bytes 32768 | tf_op jit(solution)/shard_map/jit(argsort)/sort | solution.py:84
  253.7 0.1 copy.70
  253.8 0.1 reshape.437
  254.0 1.1 gather_fusion.1
  255.2 0.7 gather_fusion.3
  256.0 0.3 copy.77
  256.2 0.7 gather_fusion.2
  257.1 0.8 pad_maximum_fusion
  257.9 71.8 %reduce-scatter.5.cloned.1.call-done = bf16[64,1,4096]{2,0,1:T(8,128)(2,1)} async-done(((bf16[1024,1,4096]{2,0,1:T(8,128)(2,1)}), bf16[64,1,4096]{2,0,1:T(8,128)(2,1)}) %reduce-scatter.5.cloned.1.call-update) | async-done | bytes 524304 | tf_op jit(solution)/shard_map/reduce_scatter | solution.py:168
  329.7 1.1 constant_dynamic-slice_fusion
  330.9 2.2 collective-permute-start
  333.1 2.7 collective-permute-start.6
  335.8 0.1 collective-permute-start.5
  335.9 2.1 collective-permute-start.4
  338.0 1.3 collective-permute-start.3
  339.3 0.3 collective-permute-start.1
  339.6 5.4 %collective-permute-done.1 = bf16[64,1,512]{2,0,1:T(8,128)(2,1)S(1)} collective-permute-done((bf16[64,1,512]{2,0,1:T(8,128)(2,1)S(1)}, bf16[64,1,512]{2,0,1:T(8,128)(2,1)S(1)}, u32[]{:S(2)}, u32[]{:S(2)}) %collective-permute-start.1) | collective-permute-done | bytes 65568 | tf_op jit(solution)/shard_map/ppermute | solution.py:25
  345.1 0.1 collective-permute-start.2
  345.2 4.0 %collective-permute-done.2 = bf16[64,1,512]{2,0,1:T(8,128)(2,1)S(1)} collective-permute-done((bf16[64,1,512]{2,0,1:T(8,128)(2,1)S(1)}, bf16[64,1,512]{2,0,1:T(8,128)(2,1)S(1)}, u32[]{:S(2)}, u32[]{:S(2)}) %collective-permute-start.2) | collective-permute-done | bytes 65568 | tf_op jit(solution)/shard_map/ppermute | solution.py:25
  349.3 0.3 copy.74
  349.6 0.1 copy.75
  349.7 1.2 dynamic_update_slice.31
  350.9 1.2 gather_fusion
  352.0 0.3 reshape.443
  352.4 0.7 multiply_reduce_fusion
  353.1 0.7 add_convert_fusion
  (88 shorter events, 2.1 us)
Async XLA Ops:
  7.2 114.1 %reduce-scatter.3.cloned.1.call-start = ((), (), s32[]{:S(2)}) async-start(), calls=%async_computation.3 | async-start | bytes 1179648 | tf_op jit(solution)/shard_map/reduce_scatter | solution.py:129
  77.5 2.2 copy-start
  78.6 2.9 copy-start.4
  78.6 42.7 %copy-start.1 = (bf16[128,512]{1,0:T(8,128)(2,1)S(1)}, bf16[128,512]{1,0:T(8,128)(2,1)}, u32[]{:S(2)}) copy-start(bf16[128,512]{1,0:T(8,128)(2,1)} %param.13) | copy-start | bytes 393220
  81.4 56.8 %copy-start.3 = (f32[4096]{0:T(1024)S(1)}, f32[4096]{0:T(1024)}, u32[]{:S(2)}) copy-start(f32[4096]{0:T(1024)} %param.20) | copy-start | bytes 49156
  81.5 128.1 %all-gather.3.cloned.1.call-start = ((), (), s32[]{:S(2)}) async-start(), calls=%async_computation.4 | async-start | bytes 8912896 | tf_op jit(solution)/shard_map/all_gather | solution.py:164
  139.3 190.4 %reduce-scatter.5.cloned.1.call-start = ((), (), s32[]{:S(2)}) async-start(), calls=%async_computation.5 | async-start | bytes 8912896 | tf_op jit(solution)/shard_map/reduce_scatter | solution.py:168
  209.5 12.5 %copy-start.6 = (bf16[1,1024,4096]{2,1,0:T(8,128)(2,1)S(1)}, bf16[1,1024,4096]{2,1,0:T(8,128)(2,1)}, u32[]{:S(2)}) copy-start(bf16[1,1024,4096]{2,1,0:T(8,128)(2,1)} %all-gather.3.cloned.1.call-done) | copy-start | bytes 25165828
  209.5 24.6 %slice-start = ((s8[7340032]{0:T(1024)(128)(4,1)}), s8[4194304]{0:T(1024)(128)(4,1)S(1)}, s32[]{:S(2)}) async-start(s8[7340032]{0:T(1024)(128)(4,1)} %bitcast.133), calls=%async_computation.6 | async-start | bytes 8388608
  222.0 12.1 %slice-start.1 = ((s8[7340032]{0:T(1024)(128)(4,1)}), s8[3145728]{0:T(1024)(128)(4,1)S(1)}, s32[]{:S(2)}) async-start(s8[7340032]{0:T(1024)(128)(4,1)} %bitcast.133), calls=%async_computation.7 | async-start | bytes 6291456
  245.2 0.7 copy-start.7
  245.2 8.5 %copy-start.5 = (f32[128,2]{0,1:T(2,128)S(1)}, f32[128,2]{0,1:T(2,128)}, u32[]{:S(2)}) copy-start(f32[128,2]{0,1:T(2,128)} %param.21) | copy-start | bytes 3076
  256.2 96.8 %copy-start.2 = (bf16[128,512]{1,0:T(8,128)(2,1)S(1)}, bf16[128,512]{1,0:T(8,128)(2,1)}, u32[]{:S(2)}) copy-start(bf16[128,512]{1,0:T(8,128)(2,1)} %reduce-scatter.3.cloned.1.call-done) | copy-start | bytes 393220
  330.9 8.5 %collective-permute-start = (bf16[64,1,512]{2,0,1:T(8,128)(2,1)S(1)}, bf16[64,1,512]{2,0,1:T(8,128)(2,1)S(1)}, u32[]{:S(2)}, u32[]{:S(2)}) collective-permute-start(bf16[64,1,512]{2,0,1:T(8,128)(2,1)S(1)} %get-tuple-element.18), channel_id=1, source_target_pairs={{0,1},{1,0},{2,3},{3,2},{4,5},{5,4},{6,7},{7,6},{8,9},{9,8},{10,11... | collective-permute-start | bytes 196616 | tf_op jit(solution)/shard_map/ppermute | solution.py:25
  333.1 16.5 %collective-permute-start.6 = (bf16[64,1,512]{2,0,1:T(8,128)(2,1)S(1)}, bf16[64,1,512]{2,0,1:T(8,128)(2,1)S(1)}, u32[]{:S(2)}, u32[]{:S(2)}) collective-permute-start(bf16[64,1,512]{2,0,1:T(8,128)(2,1)S(1)} %get-tuple-element.12), channel_id=1, source_target_pairs={{0,7},{1,6},{2,5},{3,4},{4,3},{5,2},{6,1},{7,0},{8,15},{9,14},{10,... | collective-permute-start | bytes 196616 | tf_op jit(solution)/shard_map/ppermute | solution.py:25
  335.8 13.5 %collective-permute-start.5 = (bf16[64,1,512]{2,0,1:T(8,128)(2,1)S(1)}, bf16[64,1,512]{2,0,1:T(8,128)(2,1)S(1)}, u32[]{:S(2)}, u32[]{:S(2)}) collective-permute-start(bf16[64,1,512]{2,0,1:T(8,128)(2,1)S(1)} %get-tuple-element.13), channel_id=1, source_target_pairs={{0,6},{1,7},{2,4},{3,5},{4,2},{5,3},{6,0},{7,1},{8,14},{9,15},{10,... | collective-permute-start | bytes 196616 | tf_op jit(solution)/shard_map/ppermute | solution.py:25
  335.9 13.3 %collective-permute-start.4 = (bf16[64,1,512]{2,0,1:T(8,128)(2,1)S(1)}, bf16[64,1,512]{2,0,1:T(8,128)(2,1)S(1)}, u32[]{:S(2)}, u32[]{:S(2)}) collective-permute-start(bf16[64,1,512]{2,0,1:T(8,128)(2,1)S(1)} %get-tuple-element.14), channel_id=1, source_target_pairs={{0,5},{1,4},{2,7},{3,6},{4,1},{5,0},{6,3},{7,2},{8,13},{9,12},{10,... | collective-permute-start | bytes 196616 | tf_op jit(solution)/shard_map/ppermute | solution.py:25
  338.0 11.2 %collective-permute-start.3 = (bf16[64,1,512]{2,0,1:T(8,128)(2,1)S(1)}, bf16[64,1,512]{2,0,1:T(8,128)(2,1)S(1)}, u32[]{:S(2)}, u32[]{:S(2)}) collective-permute-start(bf16[64,1,512]{2,0,1:T(8,128)(2,1)S(1)} %get-tuple-element.15), channel_id=1, source_target_pairs={{0,4},{1,5},{2,6},{3,7},{4,0},{5,1},{6,2},{7,3},{8,12},{9,13},{10,... | collective-permute-start | bytes 196616 | tf_op jit(solution)/shard_map/ppermute | solution.py:25
  339.3 5.8 %collective-permute-start.1 = (bf16[64,1,512]{2,0,1:T(8,128)(2,1)S(1)}, bf16[64,1,512]{2,0,1:T(8,128)(2,1)S(1)}, u32[]{:S(2)}, u32[]{:S(2)}) collective-permute-start(bf16[64,1,512]{2,0,1:T(8,128)(2,1)S(1)} %get-tuple-element.17), channel_id=1, source_target_pairs={{0,2},{1,3},{2,0},{3,1},{4,6},{5,7},{6,4},{7,5},{8,10},{9,11},{10,... | collective-permute-start | bytes 196616 | tf_op jit(solution)/shard_map/ppermute | solution.py:25
  345.1 4.1 %collective-permute-start.2 = (bf16[64,1,512]{2,0,1:T(8,128)(2,1)S(1)}, bf16[64,1,512]{2,0,1:T(8,128)(2,1)S(1)}, u32[]{:S(2)}, u32[]{:S(2)}) collective-permute-start(bf16[64,1,512]{2,0,1:T(8,128)(2,1)S(1)} %get-tuple-element.16), channel_id=1, source_target_pairs={{0,3},{1,2},{2,1},{3,0},{4,7},{5,6},{6,5},{7,4},{8,11},{9,10},{10,... | collective-permute-start | bytes 196616 | tf_op jit(solution)/shard_map/ppermute | solution.py:25
Sparse Core Ops, SparseCore 0:
  81.6 39.6 reduce-scatter.2
  139.4 70.0 all-gather.2
  245.4 84.2 reduce-scatter.4
